TPU v7x, 512 devices: a whole 4x4x16 slice. The times are simulated.
512 devices in a mesh: phase: 16 (over x, z_hi), slab: 32 (over z_lo, y, core).
Axes of the slice: x: 4, y: 4, z: 16 (z_hi: 4, z_lo: 4; z = z_hi * 4 + z_lo), core: 2. Of those that a mesh axis runs over, the one named last changes fastest.
Arguments:
- pressure: float32 [2, 64, 32, 98304], P(None, 'phase', None, 'slab'), may hold values from -6 to 6
- mode_shapes: float32 [1024, 98304], P('phase', 'slab'), may hold values from -0.0390625 to 0.0390625
- point_weight: float32 [98304], P('slab'), may hold values from 0.5 to 2
- panel_order: int32 [8], replicated, may hold values from 0 to 7, each once
Outputs:
- influence: float32 [2, 64, 32, 1024], P(None, None, 'phase', 'slab')
Inputs may be any that keep to these rules, and one draw needn't show every extreme that they name: panel_order names each of 0 to 7 once.
All inputs are finite; a program needn't handle non-finite values.
Results may differ from a plain program's by a relative error of at most 0.00007.
Values sent between devices are 32-bit elements; how exact they have to be, the bound alone decides.
No kernel may reach another device: no remote copies, remote signals or barrier semaphores. Data moves between devices by JAX's collectives and lax.ppermute only.
A program may use at most 64 MiB of HBM per device.

v0:
```python
import math
import jax
import jax.numpy as jnp
from jax import lax
from jax.sharding import PartitionSpec as P


def blade_table(blades, count):
    phases = jnp.arange(count, dtype=jnp.int32)
    target = jnp.arange(blades, dtype=jnp.int32)
    index = target[:, None] * phases[None, :] % blades
    theta = index.astype(jnp.float32) * (2.0 * math.pi / blades)
    cosine = jnp.cos(theta)
    sine = jnp.sin(theta)
    upper = jnp.concatenate([cosine, -sine], axis=1)
    lower = jnp.concatenate([sine, cosine], axis=1)
    return jnp.concatenate([upper, lower], axis=0) * (1.0 / math.sqrt(blades))


def shards(pressure, mode_shapes, point_weight, panel_order):
    weighted = mode_shapes * point_weight[None, :]
    phase_dev = pressure.shape[1]
    excite = pressure.shape[2]
    rows = pressure.reshape(2 * phase_dev * excite, pressure.shape[3])
    partial_forces = lax.dot_general(
        rows,
        lax.all_gather(weighted, "phase", axis=0, tiled=True),
        (((1,), (1,)), ((), ())),
        precision=lax.Precision.HIGHEST,
        preferred_element_type=jnp.float32,
    )
    row_count = partial_forces.shape[0]
    panel_count = panel_order.shape[0]
    panels = partial_forces.reshape(row_count, panel_count, -1)
    selector = (panel_order[:, None] == jnp.arange(panel_count, dtype=jnp.int32)[None, :]).astype(
        jnp.float32
    )
    reordered = jnp.einsum(
        "rqc,pq->rpc", panels, selector, precision=lax.Precision.HIGHEST
    ).reshape(row_count, -1)
    slab_count = lax.axis_size("slab")
    total = lax.psum(reordered, "slab")
    keep_width = total.shape[1] // slab_count
    share = lax.dynamic_slice_in_dim(total, lax.axis_index("slab") * keep_width, keep_width, 1)
    mode_local = share.shape[1]
    forces = share.reshape(2, phase_dev, excite, mode_local)
    blades = phase_dev * lax.axis_size("phase")
    gathered = lax.all_to_all(forces, "phase", split_axis=2, concat_axis=1, tiled=True)
    table = blade_table(blades, blades)
    result = jnp.dot(
        table,
        gathered.reshape(2 * blades, -1),
        precision=lax.Precision.HIGHEST,
        preferred_element_type=jnp.float32,
    )
    result = result.reshape(2, blades, -1, mode_local)
    return result


def solution(mesh):
    placed = (P(None, "phase", None, "slab"), P("phase", "slab"), P("slab"), P())
    return jax.shard_map(
        shards,
        mesh=mesh,
        in_specs=placed,
        out_specs=P(None, None, "phase", "slab"),
        check_vma=False,
    )
```

profile of v0, /device:TPU:2, one launch (start us, length us, event | category | flops | bytes accessed | tf_op | source)
XLA Modules:
  0.0 662.7 jit_solution(11755668683219762363)
XLA Ops:
  6.5 0.0 copy-start
  6.5 0.0 copy-start.1
  6.5 0.0 all-gather.2.cloned.1.call-start
  6.5 2.3 broadcast_multiply_fusion
  8.8 0.0 all-gather.2.cloned.1.call-update
  8.8 0.0 all-reduce.2.cloned.1.call-start
  8.9 307.7 %all-gather.2.cloned.1.call-done = f32[1024,3072]{1,0:T(8,128)} async-done(((f32[64,3072]{1,0:T(8,128)}), f32[1024,3072]{1,0:T(8,128)}) %all-gather.2.cloned.1.call-update) | async-done | bytes 12582928 | tf_op jit(solution)/shard_map/all_gather | solution.py:27
  316.6 0.0 copy-done
  316.6 13.5 %fusion.12 = f32[1024,256]{1,0:T(8,128)} fusion(f32[1024,3072]{1,0:T(8,128)} %all-gather.2.cloned.1.call-done, f32[256,3072]{1,0:T(8,128)S(1)} %bitcast.31), kind=kOutput, calls=%fused_computation.19 | convolution fusion | flops 9663676416 | bytes 16777216 | tf_op jit(solution)/shard_map/dot_general | solution.py:25
  330.1 2.5 copy.13
  332.6 0.0 copy-done.1
  332.6 2.9 convolution_bitcast_fusion
  335.5 2.5 copy.20
  338.0 0.0 all-reduce.2.cloned.1.call-update
  338.1 0.1 fusion.6
  338.2 285.0 %all-reduce.2.cloned.1.call-done = f32[256,1024]{0,1:T(8,128)} async-done(((f32[256,1024]{0,1:T(8,128)}), f32[256,1024]{0,1:T(8,128)}) %all-reduce.2.cloned.1.call-update) | async-done | bytes 1048592 | tf_op jit(solution)/shard_map/psum | solution.py:42
  623.2 0.8 constant_dynamic-slice_fusion
  624.0 0.1 reshape.32
  624.1 0.1 copy.15
  624.3 0.8 reshape.37
  625.0 14.8 %all-to-all-start = ((f32[16,1,512]{2,1,0:T(1,128)}), f32[16,1,512]{2,1,0:T(1,128)S(1)}, u32[]{:S(2)}, u32[]{:S(2)}) async-start(f32[16,1,512]{2,1,0:T(1,128)} %reshape.37), calls=%async_computation | async-start | bytes 65536 | tf_op jit(solution)/shard_map/all_to_all | solution.py:48
  639.8 0.1 fusion.8
  639.9 0.1 maximum_multiply_fusion
  640.0 13.2 %all-to-all-done = f32[16,1,512]{2,1,0:T(1,128)S(1)} async-done(((f32[16,1,512]{2,1,0:T(1,128)}), f32[16,1,512]{2,1,0:T(1,128)S(1)}, u32[]{:S(2)}, u32[]{:S(2)}) %all-to-all-start) | async-done | bytes 32800 | tf_op jit(solution)/shard_map/all_to_all | solution.py:48
  653.2 0.5 broadcast.24
  653.7 0.7 reduce
  654.5 0.1 reshape.38
  654.7 0.1 reshape.33
  654.8 0.1 copy.18
  654.9 1.0 fusion.13
  (2 shorter events, 0.1 us)
Async XLA Ops:
  6.5 310.1 %copy-start = (f32[2,4,32,3072]{3,2,1,0:T(8,128)S(1)}, f32[2,4,32,3072]{3,2,1,0:T(8,128)}, u32[]{:S(2)}) copy-start(f32[2,4,32,3072]{3,2,1,0:T(8,128)} %param.4) | copy-start | bytes 9437188
  6.5 326.1 %copy-start.1 = (s32[8]{0:T(128)S(1)}, s32[8]{0:T(128)}, u32[]{:S(2)}) copy-start(s32[8]{0:T(128)} %param.7) | copy-start | bytes 100
  6.5 310.1 %all-gather.2.cloned.1.call-start = ((), (), s32[]{:S(2)}) async-start(), calls=%async_computation.1 | async-start | bytes 13369344 | tf_op jit(solution)/shard_map/all_gather | solution.py:27
  8.8 614.4 %all-reduce.2.cloned.1.call-start = ((), (), s32[]{:S(2)}) async-start(), calls=%async_computation.2 | async-start | bytes 2097152 | tf_op jit(solution)/shard_map/psum | solution.py:42
  625.0 28.2 %all-to-all-start = ((f32[16,1,512]{2,1,0:T(1,128)}), f32[16,1,512]{2,1,0:T(1,128)S(1)}, u32[]{:S(2)}, u32[]{:S(2)}) async-start(f32[16,1,512]{2,1,0:T(1,128)} %reshape.37), calls=%async_computation | async-start | bytes 65536 | tf_op jit(solution)/shard_map/all_to_all | solution.py:48
Sparse Core Ops, SparseCore 0:
  10.4 306.1 all-gather.1
  338.2 285.0 all-reduce.1
where the time goes:
time: 663 us
  waiting for transfers between devices  606 us (91%)
  matrix products  17.3 us (3%)
  starting transfers between devices  14.8 us (2%)
  between operations  13.5 us (2%)
  local copies, waits for them, and re-layouts  7.73 us (1%)
    all_gather x1, waiting for transfers between devices, shards(): lax.all_gather(weighted, 'phase', axis=0, tiled=True)  308 us
    psum x1, waiting for transfers between devices, shards(): total = lax.psum(reordered, 'slab')  285 us
    all_to_all x1, starting transfers between devices, shards(): lax.all_to_all(forces, 'phase', split_axis=2, concat_axis=1, tiled=True)  14.8 us
    dot_general x1, matrix products, shards(): lax.dot_general(rows, lax.all_gather(weighted, 'phase', axis=0, tiled=Tru...  13.5 us
  transfers between devices with their start and end apart: 3, of which 3 were waited for; matrix products, arithmetic and copies ran while one was open for 0% of the time, Pallas kernels for 0%

commit v1 on v0

--- a/solution.py
+++ b/solution.py
@@ -45,7 +45,9 @@
     mode_local = share.shape[1]
     forces = share.reshape(2, phase_dev, excite, mode_local)
     blades = phase_dev * lax.axis_size("phase")
-    gathered = lax.all_to_all(forces, "phase", split_axis=2, concat_axis=1, tiled=True)
+    gathered = jnp.concatenate(
+        lax.all_to_all(jnp.stack(jnp.split(forces, lax.axis_size("phase"), 2)), "phase", 0, 0), 1
+    )
     table = blade_table(blades, blades)
     result = jnp.dot(
         table,

time: 663 us -> 677 us (1.021)
  local copies, waits for them, and re-layouts: 7.73 us -> 22.2 us
    unnamed x6 -> x21, local copies, waits for them, and re-layouts: 0.88 us -> 12.5 us
where the time goes in v1:
time: 677 us
  waiting for transfers between devices  606 us (90%)
  local copies, waits for them, and re-layouts  22.2 us (3%)
  matrix products  17.3 us (3%)
  starting transfers between devices  14.9 us (2%)
  between operations  13.5 us (2%)
    all_gather x1, waiting for transfers between devices, shards(): lax.all_gather(weighted, 'phase', axis=0, tiled=True)  308 us
    psum x1, waiting for transfers between devices, shards(): total = lax.psum(reordered, 'slab')  285 us
    all_to_all x1, starting transfers between devices, shards(): lax.all_to_all(jnp.stack(jnp.split(forces, lax.axis_size('phase'), 2)), '...  14.9 us
  transfers between devices with their start and end apart: 3, of which 3 were waited for; matrix products, arithmetic and copies ran while one was open for 0% of the time, Pallas kernels for 0%

profile of v1, /device:TPU:2, one launch (start us, length us, event | category | flops | bytes accessed | tf_op | source)
XLA Modules:
  0.0 677.0 jit_solution(8253058357911219698)
XLA Ops:
  6.5 0.0 copy-start
  6.5 0.0 all-gather.2.cloned.1.call-start
  6.5 2.3 broadcast_multiply_fusion
  8.8 0.0 all-gather.2.cloned.1.call-update
  8.8 0.0 all-reduce.2.cloned.1.call-start
  8.9 307.7 %all-gather.2.cloned.1.call-done = f32[1024,3072]{1,0:T(8,128)} async-done(((f32[64,3072]{1,0:T(8,128)}), f32[1024,3072]{1,0:T(8,128)}) %all-gather.2.cloned.1.call-update) | async-done | bytes 12582928 | tf_op jit(solution)/shard_map/all_gather | solution.py:27
  316.6 0.0 copy-done
  316.6 13.5 %fusion.28 = f32[1024,256]{1,0:T(8,128)} fusion(f32[1024,3072]{1,0:T(8,128)} %all-gather.2.cloned.1.call-done, f32[256,3072]{1,0:T(8,128)S(1)} %bitcast.95), kind=kOutput, calls=%fused_computation.52 | convolution fusion | flops 9663676416 | bytes 16777216 | tf_op jit(solution)/shard_map/dot_general | solution.py:25
  330.1 0.0 copy-start.1
  330.1 2.6 copy.46
  332.6 0.0 copy-done.1
  332.6 2.9 convolution_bitcast_fusion
  335.5 2.5 copy.52
  338.0 0.0 all-reduce.2.cloned.1.call-update
  338.1 0.1 fusion.22
  338.2 284.8 %all-reduce.2.cloned.1.call-done = f32[256,1024]{0,1:T(8,128)} async-done(((f32[256,1024]{0,1:T(8,128)}), f32[256,1024]{0,1:T(8,128)}) %all-reduce.2.cloned.1.call-update) | async-done | bytes 1048592 | tf_op jit(solution)/shard_map/psum | solution.py:42
  623.0 0.8 constant_dynamic-slice_fusion
  623.8 0.1 reshape.31
  623.9 0.7 fusion.15
  624.6 0.8 fusion.14
  625.4 0.8 fusion.13
  626.2 0.8 fusion.12
  626.9 0.8 fusion.11
  627.7 0.8 fusion.10
  628.5 0.8 fusion.9
  629.3 0.8 fusion.8
  630.1 0.8 fusion.7
  630.9 0.8 fusion.6
  631.6 0.8 fusion.5
  632.4 0.8 fusion.4
  633.2 0.8 fusion.3
  634.0 0.8 fusion.2
  634.8 0.8 fusion.1
  635.6 0.8 fusion
  636.3 2.1 copy.48
  638.5 0.8 reshape.36
  639.2 14.9 %all-to-all-start = ((f32[16,1,512]{2,1,0:T(1,128)}), f32[16,1,512]{2,1,0:T(1,128)S(1)}, u32[]{:S(2)}, u32[]{:S(2)}) async-start(f32[16,1,512]{2,1,0:T(1,128)} %reshape.36), calls=%async_computation | async-start | bytes 65536 | tf_op jit(solution)/shard_map/all_to_all | solution.py:49
  654.1 0.1 fusion.24
  654.2 0.1 maximum_multiply_fusion
  654.3 13.2 %all-to-all-done = f32[16,1,512]{2,1,0:T(1,128)S(1)} async-done(((f32[16,1,512]{2,1,0:T(1,128)}), f32[16,1,512]{2,1,0:T(1,128)S(1)}, u32[]{:S(2)}, u32[]{:S(2)}) %all-to-all-start) | async-done | bytes 32800 | tf_op jit(solution)/shard_map/all_to_all | solution.py:49
  667.5 0.5 broadcast.24
  668.1 0.7 reduce
  668.8 0.1 reshape.37
  668.9 0.1 copy.49
  669.0 0.1 reshape_reshape.3
  669.1 0.1 copy.50
  669.2 1.0 fusion.29
  (1 shorter events, 0.0 us)
Async XLA Ops:
  6.5 310.1 %copy-start = (f32[2,4,32,3072]{3,2,1,0:T(8,128)S(1)}, f32[2,4,32,3072]{3,2,1,0:T(8,128)}, u32[]{:S(2)}) copy-start(f32[2,4,32,3072]{3,2,1,0:T(8,128)} %param.4) | copy-start | bytes 9437188
  6.5 310.1 %all-gather.2.cloned.1.call-start = ((), (), s32[]{:S(2)}) async-start(), calls=%async_computation.1 | async-start | bytes 13369344 | tf_op jit(solution)/shard_map/all_gather | solution.py:27
  8.8 614.2 %all-reduce.2.cloned.1.call-start = ((), (), s32[]{:S(2)}) async-start(), calls=%async_computation.2 | async-start | bytes 2097152 | tf_op jit(solution)/shard_map/psum | solution.py:42
  330.1 2.6 copy-start.1
  639.2 28.3 %all-to-all-start = ((f32[16,1,512]{2,1,0:T(1,128)}), f32[16,1,512]{2,1,0:T(1,128)S(1)}, u32[]{:S(2)}, u32[]{:S(2)}) async-start(f32[16,1,512]{2,1,0:T(1,128)} %reshape.36), calls=%async_computation | async-start | bytes 65536 | tf_op jit(solution)/shard_map/all_to_all | solution.py:49
Sparse Core Ops, SparseCore 0:
  10.4 306.1 all-gather.1
  338.2 284.8 all-reduce.1

commit v2 on v0

--- a/solution.py
+++ b/solution.py
@@ -22,9 +22,13 @@
     phase_dev = pressure.shape[1]
     excite = pressure.shape[2]
     rows = pressure.reshape(2 * phase_dev * excite, pressure.shape[3])
+    samples_deliver = lambda block_in, along_axis: jnp.concatenate(
+        lax.all_to_all(jnp.stack(lax.axis_size(along_axis) * [block_in], axis=0), along_axis, 0, 0),
+        axis=0,
+    )
     partial_forces = lax.dot_general(
         rows,
-        lax.all_gather(weighted, "phase", axis=0, tiled=True),
+        samples_deliver(weighted, "phase"),
         (((1,), (1,)), ((), ())),
         precision=lax.Precision.HIGHEST,
         preferred_element_type=jnp.float32,

time: 663 us -> 916 us (1.38)
  blocking collectives: 0 us -> 564 us
  waiting for transfers between devices: 606 us -> 297 us
    all_to_all x0 -> x1, blocking collectives: none -> 564 us  [shards(): lax.all_to_all(jnp.stack(lax.axis_size(along_axis) * [block_in], axis=0),...]
    all_gather x1 -> x0, waiting for transfers between devices: 308 us -> none  [shards(): lax.all_gather(weighted, 'phase', axis=0, tiled=True)]
  transfers between devices with their start and end apart: 3 -> 2, of which waited for: 3 -> 2; matrix products, arithmetic and copies ran while one was open for 0% -> 0% of each run, Pallas kernels for 0% -> 0%
where the time goes in v2:
time: 916 us
  blocking collectives  564 us (62%)
  waiting for transfers between devices  297 us (32%)
  matrix products  15.1 us (2%)
  starting transfers between devices  14.8 us (2%)
  between operations  13.5 us (1%)
  local copies, waits for them, and re-layouts  9.29 us (1%)
    all_to_all x1, blocking collectives, shards(): lax.all_to_all(jnp.stack(lax.axis_size(along_axis) * [block_in], axis=0),...  564 us
    psum x1, waiting for transfers between devices, shards(): total = lax.psum(reordered, 'slab')  284 us
  transfers between devices with their start and end apart: 2, of which 2 were waited for; matrix products, arithmetic and copies ran while one was open for 0% of the time, Pallas kernels for 0%

profile of v2, /device:TPU:2, one launch (start us, length us, event | category | flops | bytes accessed | tf_op | source)
XLA Modules:
  0.0 915.6 jit_solution(14277636013267403603)
XLA Ops:
  6.5 0.0 copy-start
  6.5 0.0 all-reduce.2.cloned.1.call-start
  6.5 1.3 broadcast_multiply_fusion
  7.9 1.6 stack.2
  9.5 563.7 %all_to_all.20 = f32[16,64,3072]{2,1,0:T(8,128)S(1)} all-to-all(f32[16,64,3072]{2,1,0:T(8,128)S(1)} %stack.2), channel_id=1, replica_groups=mesh['phase'=16,'slab'=32] {'phase'}, dimensions={0} | all-to-all | bytes 25165824 | tf_op jit(solution)/shard_map/all_to_all | solution.py:26
  573.2 0.0 copy-start.1
  573.2 0.0 copy-done
  573.2 11.2 %fusion.12 = f32[1024,256]{1,0:T(8,128)} fusion(f32[1024,3072]{1,0:T(8,128)S(1)} %bitcast.33, f32[256,3072]{1,0:T(8,128)S(1)} %bitcast.32), kind=kOutput, calls=%fused_computation.19 | convolution fusion | flops 9663676416 | bytes 16777216 | tf_op jit(solution)/shard_map/dot_general | solution.py:29
  584.4 2.5 copy.13
  587.0 0.0 copy-done.1
  587.0 2.9 convolution_bitcast_fusion
  589.9 2.5 copy.20
  592.4 0.0 all-reduce.2.cloned.1.call-update
  592.4 0.1 fusion.6
  592.6 283.6 %all-reduce.2.cloned.1.call-done = f32[256,1024]{0,1:T(8,128)} async-done(((f32[256,1024]{0,1:T(8,128)}), f32[256,1024]{0,1:T(8,128)}) %all-reduce.2.cloned.1.call-update) | async-done | bytes 1048592 | tf_op jit(solution)/shard_map/psum | solution.py:46
  876.2 0.8 constant_dynamic-slice_fusion
  876.9 0.1 reshape.38
  877.0 0.1 copy.15
  877.2 0.8 reshape.43
  877.9 14.8 %all-to-all-start.1 = ((f32[16,1,512]{2,1,0:T(1,128)}), f32[16,1,512]{2,1,0:T(1,128)S(1)}, u32[]{:S(2)}, u32[]{:S(2)}) async-start(f32[16,1,512]{2,1,0:T(1,128)} %reshape.43), calls=%async_computation.1 | async-start | bytes 65536 | tf_op jit(solution)/shard_map/all_to_all | solution.py:52
  892.7 0.1 fusion.8
  892.8 0.1 maximum_multiply_fusion
  892.9 13.2 %all-to-all-done.1 = f32[16,1,512]{2,1,0:T(1,128)S(1)} async-done(((f32[16,1,512]{2,1,0:T(1,128)}), f32[16,1,512]{2,1,0:T(1,128)S(1)}, u32[]{:S(2)}, u32[]{:S(2)}) %all-to-all-start.1) | async-done | bytes 32800 | tf_op jit(solution)/shard_map/all_to_all | solution.py:52
  906.1 0.5 broadcast.26
  906.7 0.7 reduce
  907.4 0.1 reshape.44
  907.6 0.1 reshape.39
  907.7 0.1 copy.18
  907.8 1.0 fusion.13
  (2 shorter events, 0.1 us)
Async XLA Ops:
  6.5 566.7 %copy-start = (f32[2,4,32,3072]{3,2,1,0:T(8,128)S(1)}, f32[2,4,32,3072]{3,2,1,0:T(8,128)}, u32[]{:S(2)}) copy-start(f32[2,4,32,3072]{3,2,1,0:T(8,128)} %param.4) | copy-start | bytes 9437188
  6.5 869.6 %all-reduce.2.cloned.1.call-start = ((), (), s32[]{:S(2)}) async-start(), calls=%async_computation.2 | async-start | bytes 2097152 | tf_op jit(solution)/shard_map/psum | solution.py:46
  573.2 13.8 %copy-start.1 = (s32[8]{0:T(128)S(1)}, s32[8]{0:T(128)}, u32[]{:S(2)}) copy-start(s32[8]{0:T(128)} %param.7) | copy-start | bytes 100
  877.9 28.2 %all-to-all-start.1 = ((f32[16,1,512]{2,1,0:T(1,128)}), f32[16,1,512]{2,1,0:T(1,128)S(1)}, u32[]{:S(2)}, u32[]{:S(2)}) async-start(f32[16,1,512]{2,1,0:T(1,128)} %reshape.43), calls=%async_computation.1 | async-start | bytes 65536 | tf_op jit(solution)/shard_map/all_to_all | solution.py:52
Sparse Core Ops, SparseCore 0:
  592.5 283.5 all-reduce.1
